TPU v7x, 512 devices: a whole 4x8x8 slice. The times are simulated.
512 devices in a mesh: chain: 64 (over y, z), cross: 8 (over x, core).
Axes of the slice: x: 4, y: 8, z: 8, core: 2. Of those that a mesh axis runs over, the one named last changes fastest.
Arguments:
- right_side: bfloat16 [64, 1024, 512], P('chain', 'cross'), may hold values from -6 to 6
- self_factor: bfloat16 [6, 64, 1024, 1024], P(None, 'chain', 'cross')
- lower_factor: bfloat16 [6, 64, 1024, 1024], P(None, 'chain', 'cross'), may hold values from -0.078125 to 0.078125
- upper_factor: bfloat16 [6, 64, 1024, 1024], P(None, 'chain', 'cross'), may hold values from -0.078125 to 0.078125
Outputs:
- solution: bfloat16 [64, 1024, 512], P('chain', 'cross')
All inputs are finite; a program needn't handle non-finite values.
Results may differ from a plain program's by a relative error of at most 0.014.
Values may be sent and summed in bfloat16 or wider, within the bound.
No kernel may reach another device: no remote copies, remote signals or barrier semaphores. Data moves between devices by JAX's collectives and lax.ppermute only.
A program may use at most 64 MiB of HBM per device.

v0:
```python
import jax
import jax.numpy as jnp
from jax import lax
from jax.sharding import PartitionSpec as P


def shifted(value, axis, steps):
    count = lax.axis_size(axis)
    initial, last = (max(0, -steps), min(count, count - steps))
    return lax.ppermute(value, axis, [(source, source + steps) for source in range(initial, last)])


def reach_full(piece, dist):
    lower = shifted(piece, "chain", dist)
    upper = shifted(piece, "chain", -dist)
    return (lower, upper)


def body(right_side, self_factor, lower_factor, upper_factor):
    levels = lax.axis_size("chain").bit_length() - 1
    current = right_side[0]
    for level in range(levels):
        dist = 2**level
        own_mat = self_factor[level, 0]
        low_mat = lower_factor[level, 0]
        up_mat = upper_factor[level, 0]
        whole = lax.all_gather(current, "cross", axis=0, tiled=True)
        lower, upper = reach_full(whole, dist)
        total = jnp.dot(own_mat, whole, preferred_element_type=jnp.float32)
        total = total - jnp.dot(low_mat, lower, preferred_element_type=jnp.float32)
        total = total - jnp.dot(up_mat, upper, preferred_element_type=jnp.float32)
        current = total.astype(jnp.bfloat16)
    return current[None]


def solution(mesh):
    return jax.shard_map(
        body,
        mesh=mesh,
        in_specs=(
            P("chain", "cross", None),
            P(None, "chain", "cross", None),
            P(None, "chain", "cross", None),
            P(None, "chain", "cross", None),
        ),
        out_specs=P("chain", "cross", None),
        check_vma=False,
    )
```

profile of v0, /device:TPU:1, one launch (start us, length us, event | category | flops | bytes accessed | tf_op | source)
XLA Modules:
  0.0 539.7 jit_solution(4165311589859038631)
XLA Ops:
  6.5 0.7 all-gather.18.cloned.1.call-update
  7.3 37.0 %all-gather.18.cloned.1.call-done = bf16[1,1024,512]{2,1,0:T(8,128)(2,1)} async-done(((bf16[1,128,512]{2,1,0:T(8,128)(2,1)}), bf16[1,1024,512]{2,1,0:T(8,128)(2,1)}) %all-gather.18.cloned.1.call-update) | async-done | bytes 1048592 | tf_op jit(solution)/shard_map/all_gather | solution.py:27
  44.3 3.2 collective-permute-start
  47.5 1.3 collective-permute-start.1
  48.8 1.6 fusion.33
  50.4 19.6 %collective-permute-done = bf16[1024,512]{1,0:T(8,128)(2,1)S(1)} collective-permute-done((bf16[1024,512]{1,0:T(8,128)(2,1)}, bf16[1024,512]{1,0:T(8,128)(2,1)S(1)}, u32[]{:S(2)}, u32[]{:S(2)}) %collective-permute-start) | collective-permute-done | bytes 1048608 | tf_op jit(solution)/shard_map/ppermute | solution.py:10
  70.3 3.4 collective-permute-done.1
  73.8 1.9 fusion
  75.8 30.0 %all-gather.8.cloned.1.call-done = bf16[1024,512]{1,0:T(8,128)(2,1)} async-done(((bf16[128,512]{1,0:T(8,128)(2,1)}), bf16[1024,512]{1,0:T(8,128)(2,1)}) %all-gather.8.cloned.1.call-update) | async-done | bytes 1048592 | tf_op jit(solution)/shard_map/all_gather | solution.py:27
  105.8 4.2 collective-permute-start.2
  110.1 1.3 collective-permute-start.3
  111.4 1.7 fusion.29
  113.1 19.6 %collective-permute-done.2 = bf16[1024,512]{1,0:T(8,128)(2,1)S(1)} collective-permute-done((bf16[1024,512]{1,0:T(8,128)(2,1)}, bf16[1024,512]{1,0:T(8,128)(2,1)S(1)}, u32[]{:S(2)}, u32[]{:S(2)}) %collective-permute-start.2) | collective-permute-done | bytes 1048608 | tf_op jit(solution)/shard_map/ppermute | solution.py:10
  132.7 0.5 convolution_subtract_fusion.9
  133.1 30.1 %collective-permute-done.3 = bf16[1024,512]{1,0:T(8,128)(2,1)S(1)} collective-permute-done((bf16[1024,512]{1,0:T(8,128)(2,1)}, bf16[1024,512]{1,0:T(8,128)(2,1)S(1)}, u32[]{:S(2)}, u32[]{:S(2)}) %collective-permute-start.3) | collective-permute-done | bytes 1048608 | tf_op jit(solution)/shard_map/ppermute | solution.py:10
  163.2 2.1 fusion.10
  165.4 25.3 %all-gather.10.cloned.1.call-done = bf16[1024,512]{0,1:T(8,128)(2,1)} async-done(((bf16[128,512]{0,1:T(8,128)(2,1)}), bf16[1024,512]{0,1:T(8,128)(2,1)}) %all-gather.10.cloned.1.call-update) | async-done | bytes 1048592 | tf_op jit(solution)/shard_map/all_gather | solution.py:27
  190.7 7.8 %collective-permute-start.4 = (bf16[1024,512]{0,1:T(8,128)(2,1)}, bf16[1024,512]{0,1:T(8,128)(2,1)S(1)}, u32[]{:S(2)}, u32[]{:S(2)}) collective-permute-start(bf16[1024,512]{0,1:T(8,128)(2,1)} %all-gather.10.cloned.1.call-done), channel_id=1, source_target_pairs={{0,32},{8,40},{16,48},{24,56},{32,64},{40,72},{48,80},{56,88},{64,... | collective-permute-start | bytes 3145736 | tf_op jit(solution)/shard_map/ppermute | solution.py:10
  198.5 1.3 collective-permute-start.5
  199.8 1.7 fusion.25
  201.4 65.5 %collective-permute-done.4 = bf16[1024,512]{0,1:T(8,128)(2,1)S(1)} collective-permute-done((bf16[1024,512]{0,1:T(8,128)(2,1)}, bf16[1024,512]{0,1:T(8,128)(2,1)S(1)}, u32[]{:S(2)}, u32[]{:S(2)}) %collective-permute-start.4) | collective-permute-done | bytes 1048608 | tf_op jit(solution)/shard_map/ppermute | solution.py:10
  267.0 0.4 convolution_subtract_fusion.7
  267.4 2.0 fusion.9
  269.5 54.1 %all-gather.12.cloned.1.call-done = bf16[1024,512]{0,1:T(8,128)(2,1)} async-done(((bf16[128,512]{0,1:T(8,128)(2,1)}), bf16[1024,512]{0,1:T(8,128)(2,1)}) %all-gather.12.cloned.1.call-update) | async-done | bytes 1048592 | tf_op jit(solution)/shard_map/all_gather | solution.py:27
  323.7 3.2 collective-permute-start.6
  326.8 1.3 collective-permute-start.7
  328.1 1.7 fusion.21
  329.8 19.5 %collective-permute-done.6 = bf16[1024,512]{0,1:T(8,128)(2,1)S(1)} collective-permute-done((bf16[1024,512]{0,1:T(8,128)(2,1)}, bf16[1024,512]{0,1:T(8,128)(2,1)S(1)}, u32[]{:S(2)}, u32[]{:S(2)}) %collective-permute-start.6) | collective-permute-done | bytes 1048608 | tf_op jit(solution)/shard_map/ppermute | solution.py:10
  349.3 0.4 convolution_subtract_fusion.5
  349.8 3.3 collective-permute-done.7
  353.1 2.0 fusion.8
  355.2 31.2 %all-gather.14.cloned.1.call-done = bf16[1024,512]{0,1:T(8,128)(2,1)} async-done(((bf16[128,512]{0,1:T(8,128)(2,1)}), bf16[1024,512]{0,1:T(8,128)(2,1)}) %all-gather.14.cloned.1.call-update) | async-done | bytes 1048592 | tf_op jit(solution)/shard_map/all_gather | solution.py:27
  386.4 4.1 collective-permute-start.8
  390.5 1.3 collective-permute-start.9
  391.8 1.7 fusion.17
  393.5 19.6 %collective-permute-done.8 = bf16[1024,512]{0,1:T(8,128)(2,1)S(1)} collective-permute-done((bf16[1024,512]{0,1:T(8,128)(2,1)}, bf16[1024,512]{0,1:T(8,128)(2,1)S(1)}, u32[]{:S(2)}, u32[]{:S(2)}) %collective-permute-start.8) | collective-permute-done | bytes 1048608 | tf_op jit(solution)/shard_map/ppermute | solution.py:10
  413.1 0.4 convolution_subtract_fusion.3
  413.5 28.4 %collective-permute-done.9 = bf16[1024,512]{0,1:T(8,128)(2,1)S(1)} collective-permute-done((bf16[1024,512]{0,1:T(8,128)(2,1)}, bf16[1024,512]{0,1:T(8,128)(2,1)S(1)}, u32[]{:S(2)}, u32[]{:S(2)}) %collective-permute-start.9) | collective-permute-done | bytes 1048608 | tf_op jit(solution)/shard_map/ppermute | solution.py:10
  441.9 2.0 fusion.7
  444.0 28.5 %all-gather.16.cloned.1.call-done = bf16[1024,512]{0,1:T(8,128)(2,1)} async-done(((bf16[128,512]{0,1:T(8,128)(2,1)}), bf16[1024,512]{0,1:T(8,128)(2,1)}) %all-gather.16.cloned.1.call-update) | async-done | bytes 1048592 | tf_op jit(solution)/shard_map/all_gather | solution.py:27
  472.5 7.1 %collective-permute-start.10 = (bf16[1024,512]{0,1:T(8,128)(2,1)}, bf16[1024,512]{0,1:T(8,128)(2,1)S(1)}, u32[]{:S(2)}, u32[]{:S(2)}) collective-permute-start(bf16[1024,512]{0,1:T(8,128)(2,1)} %all-gather.16.cloned.1.call-done), channel_id=1, source_target_pairs={{0,256},{8,264},{16,272},{24,280},{32,288},{40,296},{48,304},{56,3... | collective-permute-start | bytes 3145736 | tf_op jit(solution)/shard_map/ppermute | solution.py:10
  479.7 1.3 collective-permute-start.11
  481.0 1.7 fusion.13
  482.6 32.1 %collective-permute-done.10 = bf16[1024,512]{0,1:T(8,128)(2,1)S(1)} collective-permute-done((bf16[1024,512]{0,1:T(8,128)(2,1)}, bf16[1024,512]{0,1:T(8,128)(2,1)S(1)}, u32[]{:S(2)}, u32[]{:S(2)}) %collective-permute-start.10) | collective-permute-done | bytes 1048608 | tf_op jit(solution)/shard_map/ppermute | solution.py:10
  514.7 0.4 convolution_subtract_fusion.1
  515.1 15.6 %collective-permute-done.11 = bf16[1024,512]{0,1:T(8,128)(2,1)S(1)} collective-permute-done((bf16[1024,512]{0,1:T(8,128)(2,1)}, bf16[1024,512]{0,1:T(8,128)(2,1)S(1)}, u32[]{:S(2)}, u32[]{:S(2)}) %collective-permute-start.11) | collective-permute-done | bytes 1048608 | tf_op jit(solution)/shard_map/ppermute | solution.py:10
  530.7 1.4 fusion.6
  532.1 0.8 copy.5
  (17 shorter events, 0.6 us)
Async XLA Ops:
  6.5 63.5 %copy-start = (bf16[6,1,128,1024]{3,2,1,0:T(8,128)(2,1)S(1)}, bf16[6,1,128,1024]{3,2,1,0:T(8,128)(2,1)}, u32[]{:S(2)}) copy-start(bf16[6,1,128,1024]{3,2,1,0:T(8,128)(2,1)} %param.6) | copy-start | bytes 4718596
  6.5 37.8 %all-gather.18.cloned.1.call-start = ((), (), s32[]{:S(2)}) async-start(), calls=%async_computation.5 | async-start | bytes 1179648 | tf_op jit(solution)/shard_map/all_gather | solution.py:27
  7.3 98.6 %all-gather.8.cloned.1.call-start = ((), (), s32[]{:S(2)}) async-start(), calls=%async_computation | async-start | bytes 1179648 | tf_op jit(solution)/shard_map/all_gather | solution.py:27
  44.3 25.7 %collective-permute-start = (bf16[1024,512]{1,0:T(8,128)(2,1)}, bf16[1024,512]{1,0:T(8,128)(2,1)S(1)}, u32[]{:S(2)}, u32[]{:S(2)}) collective-permute-start(bf16[1024,512]{1,0:T(8,128)(2,1)} %bitcast.86), channel_id=1, source_target_pairs={{0,8},{8,16},{16,24},{24,32},{32,40},{40,48},{48,56},{56,64},{64,7... | collective-permute-start | bytes 3145736 | tf_op jit(solution)/shard_map/ppermute | solution.py:10
  47.5 26.3 %collective-permute-start.1 = (bf16[1024,512]{1,0:T(8,128)(2,1)}, bf16[1024,512]{1,0:T(8,128)(2,1)S(1)}, u32[]{:S(2)}, u32[]{:S(2)}) collective-permute-start(bf16[1024,512]{1,0:T(8,128)(2,1)} %bitcast.87), channel_id=1, source_target_pairs={{8,0},{16,8},{24,16},{32,24},{40,32},{48,40},{56,48},{64,56},{72,6... | collective-permute-start | bytes 3145736 | tf_op jit(solution)/shard_map/ppermute | solution.py:10
  50.4 61.0 %copy-start.1 = (bf16[6,1,128,1024]{3,2,1,0:T(8,128)(2,1)S(1)}, bf16[6,1,128,1024]{3,2,1,0:T(8,128)(2,1)}, u32[]{:S(2)}) copy-start(bf16[6,1,128,1024]{3,2,1,0:T(8,128)(2,1)} %param.5) | copy-start | bytes 4718596
  75.7 115.0 %all-gather.10.cloned.1.call-start = ((), (), s32[]{:S(2)}) async-start(), calls=%async_computation.1 | async-start | bytes 1179648 | tf_op jit(solution)/shard_map/all_gather | solution.py:27
  105.8 26.8 %collective-permute-start.2 = (bf16[1024,512]{1,0:T(8,128)(2,1)}, bf16[1024,512]{1,0:T(8,128)(2,1)S(1)}, u32[]{:S(2)}, u32[]{:S(2)}) collective-permute-start(bf16[1024,512]{1,0:T(8,128)(2,1)} %all-gather.8.cloned.1.call-done), channel_id=1, source_target_pairs={{0,16},{8,24},{16,32},{24,40},{32,48},{40,56},{48,64},{56,72},{64,... | collective-permute-start | bytes 3145736 | tf_op jit(solution)/shard_map/ppermute | solution.py:10
  110.1 53.2 %collective-permute-start.3 = (bf16[1024,512]{1,0:T(8,128)(2,1)}, bf16[1024,512]{1,0:T(8,128)(2,1)S(1)}, u32[]{:S(2)}, u32[]{:S(2)}) collective-permute-start(bf16[1024,512]{1,0:T(8,128)(2,1)} %all-gather.8.cloned.1.call-done), channel_id=1, source_target_pairs={{16,0},{24,8},{32,16},{40,24},{48,32},{56,40},{64,48},{72,56},{80,... | collective-permute-start | bytes 3145736 | tf_op jit(solution)/shard_map/ppermute | solution.py:10
  165.3 158.3 %all-gather.12.cloned.1.call-start = ((), (), s32[]{:S(2)}) async-start(), calls=%async_computation.2 | async-start | bytes 1179648 | tf_op jit(solution)/shard_map/all_gather | solution.py:27
  190.7 76.3 %collective-permute-start.4 = (bf16[1024,512]{0,1:T(8,128)(2,1)}, bf16[1024,512]{0,1:T(8,128)(2,1)S(1)}, u32[]{:S(2)}, u32[]{:S(2)}) collective-permute-start(bf16[1024,512]{0,1:T(8,128)(2,1)} %all-gather.10.cloned.1.call-done), channel_id=1, source_target_pairs={{0,32},{8,40},{16,48},{24,56},{32,64},{40,72},{48,80},{56,88},{64,... | collective-permute-start | bytes 3145736 | tf_op jit(solution)/shard_map/ppermute | solution.py:10
  198.5 69.0 %collective-permute-start.5 = (bf16[1024,512]{0,1:T(8,128)(2,1)}, bf16[1024,512]{0,1:T(8,128)(2,1)S(1)}, u32[]{:S(2)}, u32[]{:S(2)}) collective-permute-start(bf16[1024,512]{0,1:T(8,128)(2,1)} %all-gather.10.cloned.1.call-done), channel_id=1, source_target_pairs={{32,0},{40,8},{48,16},{56,24},{64,32},{72,40},{80,48},{88,56},{96,... | collective-permute-start | bytes 3145736 | tf_op jit(solution)/shard_map/ppermute | solution.py:10
  269.5 116.9 %all-gather.14.cloned.1.call-start = ((), (), s32[]{:S(2)}) async-start(), calls=%async_computation.3 | async-start | bytes 1179648 | tf_op jit(solution)/shard_map/all_gather | solution.py:27
  323.7 25.7 %collective-permute-start.6 = (bf16[1024,512]{0,1:T(8,128)(2,1)}, bf16[1024,512]{0,1:T(8,128)(2,1)S(1)}, u32[]{:S(2)}, u32[]{:S(2)}) collective-permute-start(bf16[1024,512]{0,1:T(8,128)(2,1)} %all-gather.12.cloned.1.call-done), channel_id=1, source_target_pairs={{0,64},{8,72},{16,80},{24,88},{32,96},{40,104},{48,112},{56,120},{... | collective-permute-start | bytes 3145736 | tf_op jit(solution)/shard_map/ppermute | solution.py:10
  326.8 26.3 %collective-permute-start.7 = (bf16[1024,512]{0,1:T(8,128)(2,1)}, bf16[1024,512]{0,1:T(8,128)(2,1)S(1)}, u32[]{:S(2)}, u32[]{:S(2)}) collective-permute-start(bf16[1024,512]{0,1:T(8,128)(2,1)} %all-gather.12.cloned.1.call-done), channel_id=1, source_target_pairs={{64,0},{72,8},{80,16},{88,24},{96,32},{104,40},{112,48},{120,56},{... | collective-permute-start | bytes 3145736 | tf_op jit(solution)/shard_map/ppermute | solution.py:10
  355.2 117.4 %all-gather.16.cloned.1.call-start = ((), (), s32[]{:S(2)}) async-start(), calls=%async_computation.4 | async-start | bytes 1179648 | tf_op jit(solution)/shard_map/all_gather | solution.py:27
  386.4 26.6 %collective-permute-start.8 = (bf16[1024,512]{0,1:T(8,128)(2,1)}, bf16[1024,512]{0,1:T(8,128)(2,1)S(1)}, u32[]{:S(2)}, u32[]{:S(2)}) collective-permute-start(bf16[1024,512]{0,1:T(8,128)(2,1)} %all-gather.14.cloned.1.call-done), channel_id=1, source_target_pairs={{0,128},{8,136},{16,144},{24,152},{32,160},{40,168},{48,176},{56,1... | collective-permute-start | bytes 3145736 | tf_op jit(solution)/shard_map/ppermute | solution.py:10
  390.5 51.5 %collective-permute-start.9 = (bf16[1024,512]{0,1:T(8,128)(2,1)}, bf16[1024,512]{0,1:T(8,128)(2,1)S(1)}, u32[]{:S(2)}, u32[]{:S(2)}) collective-permute-start(bf16[1024,512]{0,1:T(8,128)(2,1)} %all-gather.14.cloned.1.call-done), channel_id=1, source_target_pairs={{128,0},{136,8},{144,16},{152,24},{160,32},{168,40},{176,48},{184,... | collective-permute-start | bytes 3145736 | tf_op jit(solution)/shard_map/ppermute | solution.py:10
  472.5 42.2 %collective-permute-start.10 = (bf16[1024,512]{0,1:T(8,128)(2,1)}, bf16[1024,512]{0,1:T(8,128)(2,1)S(1)}, u32[]{:S(2)}, u32[]{:S(2)}) collective-permute-start(bf16[1024,512]{0,1:T(8,128)(2,1)} %all-gather.16.cloned.1.call-done), channel_id=1, source_target_pairs={{0,256},{8,264},{16,272},{24,280},{32,288},{40,296},{48,304},{56,3... | collective-permute-start | bytes 3145736 | tf_op jit(solution)/shard_map/ppermute | solution.py:10
  479.7 51.0 %collective-permute-start.11 = (bf16[1024,512]{0,1:T(8,128)(2,1)}, bf16[1024,512]{0,1:T(8,128)(2,1)S(1)}, u32[]{:S(2)}, u32[]{:S(2)}) collective-permute-start(bf16[1024,512]{0,1:T(8,128)(2,1)} %all-gather.16.cloned.1.call-done), channel_id=1, source_target_pairs={{256,0},{264,8},{272,16},{280,24},{288,32},{296,40},{304,48},{312,... | collective-permute-start | bytes 3145736 | tf_op jit(solution)/shard_map/ppermute | solution.py:10
Sparse Core Ops, SparseCore 0:
  9.5 34.7 all-gather.17
  75.8 29.9 all-gather.7
  165.5 25.1 all-gather.9
  269.6 53.9 all-gather.11
  355.3 31.0 all-gather.13
  444.1 28.3 all-gather.15
where the time goes:
time: 540 us
  waiting for transfers between devices  464 us (86%)
  starting transfers between devices  37.5 us (7%)
  matrix products  24.1 us (4%)
  between operations  13.7 us (3%)
    ppermute x12, waiting for transfers between devices, shifted(): lax.ppermute(value, axis, [(source, source + steps) for source in range(i...  257 us
    all_gather x6, waiting for transfers between devices, body(): whole = lax.all_gather(current, 'cross', axis=0, tiled=True)  206 us
    ppermute x12, starting transfers between devices, shifted(): lax.ppermute(value, axis, [(source, source + steps) for source in range(i...  37.3 us
    dot_general x6, matrix products, body(): total = total - jnp.dot(up_mat, upper, preferred_element_type=jnp.float32)  11.5 us
  transfers between devices with their start and end apart: 18, of which 17 were waited for; matrix products, arithmetic and copies ran while one was open for 2% of the time, Pallas kernels for 0%

commit v1 on v0

--- a/solution.py
+++ b/solution.py
@@ -2,6 +2,27 @@
 import jax.numpy as jnp
 from jax import lax
 from jax.sharding import PartitionSpec as P
+
+
+def gather_around(x, axis, dim):
+    size, index, rows = (lax.axis_size(axis), lax.axis_index(axis), x.shape[dim])
+    forward = [(i, (i + 1) % size) for i in range(size)]
+    left = [(i, (i - 1) % size) for i in range(size)]
+    filled = jnp.zeros((*x.shape[:dim], size * rows, *x.shape[dim + 1 :]), x.dtype)
+    filled = lax.dynamic_update_slice_in_dim(filled, x, index * rows, axis=dim)
+    from_left = from_right = x
+    half = size // 2
+    for step in range(1, half + 1):
+        from_left = lax.ppermute(from_left, axis, forward)
+        filled = lax.dynamic_update_slice_in_dim(
+            filled, from_left, (index - step) % size * rows, axis=dim
+        )
+        if step < size - half:
+            from_right = lax.ppermute(from_right, axis, left)
+            filled = lax.dynamic_update_slice_in_dim(
+                filled, from_right, (index + step) % size * rows, axis=dim
+            )
+    return filled
 
 
 def shifted(value, axis, steps):
@@ -24,7 +45,7 @@
         own_mat = self_factor[level, 0]
         low_mat = lower_factor[level, 0]
         up_mat = upper_factor[level, 0]
-        whole = lax.all_gather(current, "cross", axis=0, tiled=True)
+        whole = gather_around(current, "cross", 0)
         lower, upper = reach_full(whole, dist)
         total = jnp.dot(own_mat, whole, preferred_element_type=jnp.float32)
         total = total - jnp.dot(low_mat, lower, preferred_element_type=jnp.float32)

time: 540 us -> 448 us (0.83)
  the two profiles are of different devices: /device:TPU:1 before, /device:TPU:32 now
where the time goes in v1:
time: 448 us
  waiting for transfers between devices  336 us (75%)
  starting transfers between devices  98.1 us (22%)
  matrix products  8.2 us (2%)
  local copies, waits for them, and re-layouts  4.99 us (1%)
    ppermute x12, waiting for transfers between devices, shifted(): lax.ppermute(value, axis, [(source, source + steps) for source in range(i...  258 us
    ppermute x24, waiting for transfers between devices, gather_around(): from_left = lax.ppermute(from_left, axis, forward)  77.7 us
    ppermute x18, starting transfers between devices, gather_around(): from_right = lax.ppermute(from_right, axis, left)  53.2 us
    ppermute x12, starting transfers between devices, shifted(): lax.ppermute(value, axis, [(source, source + steps) for source in range(i...  44.7 us
  transfers between devices with their start and end apart: 54, of which 35 were waited for; matrix products, arithmetic and copies ran while one was open for 1% of the time, Pallas kernels for 0%

profile of v1, /device:TPU:32, one launch (start us, length us, event | category | flops | bytes accessed | tf_op | source)
XLA Modules:
  0.0 448.0 jit_solution(862060390657990457)
XLA Ops:
  0.0 3.0 collective-permute-start.1
  6.2 2.9 collective-permute-start.3
  11.9 3.0 collective-permute-start.5
  17.7 5.4 %collective-permute-done.6 = bf16[128,512]{1,0:T(8,128)(2,1)S(1)} collective-permute-done((bf16[128,512]{1,0:T(8,128)(2,1)S(1)}, bf16[128,512]{1,0:T(8,128)(2,1)S(1)}, u32[]{:S(2)}, u32[]{:S(2)}) %collective-permute-start.6) | collective-permute-done | bytes 131104 | tf_op jit(solution)/shard_map/ppermute | solution.py:16
  23.2 11.0 %collective-permute-start.8 = (bf16[1024,512]{0,1:T(8,128)(2,1)S(1)}, bf16[1024,512]{0,1:T(8,128)(2,1)S(1)}, u32[]{:S(2)}, u32[]{:S(2)}) collective-permute-start(bf16[1024,512]{0,1:T(8,128)(2,1)S(1)} %constant_dynamic-update-slice_fusion.40), channel_id=1, source_target_pairs={{8,0},{16,8},{24,16},{32,24},{40,32},{48,40},{56,48},{64,56},{72,6... | collective-permute-start | bytes 3145736 | tf_op jit(solution)/shard_map/ppermute | solution.py:31
  36.1 16.4 %collective-permute-done.8 = bf16[1024,512]{0,1:T(8,128)(2,1)S(1)} collective-permute-done((bf16[1024,512]{0,1:T(8,128)(2,1)S(1)}, bf16[1024,512]{0,1:T(8,128)(2,1)S(1)}, u32[]{:S(2)}, u32[]{:S(2)}) %collective-permute-start.8) | collective-permute-done | bytes 1048608 | tf_op jit(solution)/shard_map/ppermute | solution.py:31
  53.0 7.0 %collective-permute-done.7 = bf16[1024,512]{0,1:T(8,128)(2,1)S(1)} collective-permute-done((bf16[1024,512]{0,1:T(8,128)(2,1)S(1)}, bf16[1024,512]{0,1:T(8,128)(2,1)S(1)}, u32[]{:S(2)}, u32[]{:S(2)}) %collective-permute-start.7) | collective-permute-done | bytes 1048608 | tf_op jit(solution)/shard_map/ppermute | solution.py:31
  61.1 2.9 collective-permute-start.10
  64.0 2.6 collective-permute-done.9
  66.7 3.0 collective-permute-start.12
  69.7 2.5 collective-permute-done.11
  72.3 3.0 collective-permute-start.14
  78.0 5.5 %collective-permute-done.15 = bf16[128,512]{0,1:T(8,128)(2,1)S(1)} collective-permute-done((bf16[128,512]{0,1:T(8,128)(2,1)S(1)}, bf16[128,512]{0,1:T(8,128)(2,1)S(1)}, u32[]{:S(2)}, u32[]{:S(2)}) %collective-permute-start.15) | collective-permute-done | bytes 131104 | tf_op jit(solution)/shard_map/ppermute | solution.py:16
  85.4 4.8 %collective-permute-start.16 = (bf16[1024,512]{0,1:T(8,128)(2,1)S(1)}, bf16[1024,512]{0,1:T(8,128)(2,1)S(1)}, u32[]{:S(2)}, u32[]{:S(2)}) collective-permute-start(bf16[1024,512]{0,1:T(8,128)(2,1)S(1)} %constant_dynamic-update-slice_fusion.32), channel_id=1, source_target_pairs={{0,16},{8,24},{16,32},{24,40},{32,48},{40,56},{48,64},{56,72},{64,... | collective-permute-start | bytes 3145736 | tf_op jit(solution)/shard_map/ppermute | solution.py:31
  90.3 39.5 %collective-permute-done.17 = bf16[1024,512]{0,1:T(8,128)(2,1)S(1)} collective-permute-done((bf16[1024,512]{0,1:T(8,128)(2,1)S(1)}, bf16[1024,512]{0,1:T(8,128)(2,1)S(1)}, u32[]{:S(2)}, u32[]{:S(2)}) %collective-permute-start.17) | collective-permute-done | bytes 1048608 | tf_op jit(solution)/shard_map/ppermute | solution.py:31
  130.2 4.1 collective-permute-done.16
  135.4 2.9 collective-permute-start.19
  138.3 2.6 collective-permute-done.18
  141.0 3.0 collective-permute-start.21
  146.6 3.0 collective-permute-start.23
  152.3 5.5 %collective-permute-done.24 = bf16[128,512]{0,1:T(8,128)(2,1)S(1)} collective-permute-done((bf16[128,512]{0,1:T(8,128)(2,1)S(1)}, bf16[128,512]{0,1:T(8,128)(2,1)S(1)}, u32[]{:S(2)}, u32[]{:S(2)}) %collective-permute-start.24) | collective-permute-done | bytes 131104 | tf_op jit(solution)/shard_map/ppermute | solution.py:16
  159.7 7.8 %collective-permute-start.25 = (bf16[1024,512]{0,1:T(8,128)(2,1)S(1)}, bf16[1024,512]{0,1:T(8,128)(2,1)S(1)}, u32[]{:S(2)}, u32[]{:S(2)}) collective-permute-start(bf16[1024,512]{0,1:T(8,128)(2,1)S(1)} %constant_dynamic-update-slice_fusion.24), channel_id=1, source_target_pairs={{0,32},{8,40},{16,48},{24,56},{32,64},{40,72},{48,80},{56,88},{64,... | collective-permute-start | bytes 3145736 | tf_op jit(solution)/shard_map/ppermute | solution.py:31
  167.6 82.4 %collective-permute-done.26 = bf16[1024,512]{0,1:T(8,128)(2,1)S(1)} collective-permute-done((bf16[1024,512]{0,1:T(8,128)(2,1)S(1)}, bf16[1024,512]{0,1:T(8,128)(2,1)S(1)}, u32[]{:S(2)}, u32[]{:S(2)}) %collective-permute-start.26) | collective-permute-done | bytes 1048608 | tf_op jit(solution)/shard_map/ppermute | solution.py:31
  251.5 2.9 collective-permute-start.28
  254.4 2.6 collective-permute-done.27
  257.1 3.0 collective-permute-start.30
  260.1 2.5 collective-permute-done.29
  262.7 3.0 collective-permute-start.32
  268.4 5.5 %collective-permute-done.33 = bf16[128,512]{0,1:T(8,128)(2,1)S(1)} collective-permute-done((bf16[128,512]{0,1:T(8,128)(2,1)S(1)}, bf16[128,512]{0,1:T(8,128)(2,1)S(1)}, u32[]{:S(2)}, u32[]{:S(2)}) %collective-permute-start.33) | collective-permute-done | bytes 131104 | tf_op jit(solution)/shard_map/ppermute | solution.py:16
  275.9 3.9 collective-permute-start.34
  279.8 16.8 %collective-permute-done.35 = bf16[1024,512]{0,1:T(8,128)(2,1)S(1)} collective-permute-done((bf16[1024,512]{0,1:T(8,128)(2,1)S(1)}, bf16[1024,512]{0,1:T(8,128)(2,1)S(1)}, u32[]{:S(2)}, u32[]{:S(2)}) %collective-permute-start.35) | collective-permute-done | bytes 1048608 | tf_op jit(solution)/shard_map/ppermute | solution.py:31
  297.1 2.7 collective-permute-done.34
  300.9 2.9 collective-permute-start.37
  303.8 2.6 collective-permute-done.36
  306.5 3.0 collective-permute-start.39
  312.1 3.0 collective-permute-start.41
  317.8 5.5 %collective-permute-done.42 = bf16[128,512]{0,1:T(8,128)(2,1)S(1)} collective-permute-done((bf16[128,512]{0,1:T(8,128)(2,1)S(1)}, bf16[128,512]{0,1:T(8,128)(2,1)S(1)}, u32[]{:S(2)}, u32[]{:S(2)}) %collective-permute-start.42) | collective-permute-done | bytes 131104 | tf_op jit(solution)/shard_map/ppermute | solution.py:16
  325.3 4.9 %collective-permute-start.43 = (bf16[1024,512]{0,1:T(8,128)(2,1)S(1)}, bf16[1024,512]{0,1:T(8,128)(2,1)S(1)}, u32[]{:S(2)}, u32[]{:S(2)}) collective-permute-start(bf16[1024,512]{0,1:T(8,128)(2,1)S(1)} %constant_dynamic-update-slice_fusion.8), channel_id=1, source_target_pairs={{0,128},{8,136},{16,144},{24,152},{32,160},{40,168},{48,176},{56,1... | collective-permute-start | bytes 3145736 | tf_op jit(solution)/shard_map/ppermute | solution.py:31
  330.1 39.2 %collective-permute-done.44 = bf16[1024,512]{0,1:T(8,128)(2,1)S(1)} collective-permute-done((bf16[1024,512]{0,1:T(8,128)(2,1)S(1)}, bf16[1024,512]{0,1:T(8,128)(2,1)S(1)}, u32[]{:S(2)}, u32[]{:S(2)}) %collective-permute-start.44) | collective-permute-done | bytes 1048608 | tf_op jit(solution)/shard_map/ppermute | solution.py:31
  369.8 2.7 collective-permute-done.43
  373.6 2.9 collective-permute-start.46
  376.5 2.6 collective-permute-done.45
  379.2 3.0 collective-permute-start.48
  382.2 2.5 collective-permute-done.47
  384.8 3.0 collective-permute-start.50
  390.5 5.5 %collective-permute-done.51 = bf16[128,512]{0,1:T(8,128)(2,1)S(1)} collective-permute-done((bf16[128,512]{0,1:T(8,128)(2,1)S(1)}, bf16[128,512]{0,1:T(8,128)(2,1)S(1)}, u32[]{:S(2)}, u32[]{:S(2)}) %collective-permute-start.51) | collective-permute-done | bytes 131104 | tf_op jit(solution)/shard_map/ppermute | solution.py:16
  398.7 17.8 %collective-permute-done.53 = bf16[1024,512]{0,1:T(8,128)(2,1)S(1)} collective-permute-done((bf16[1024,512]{0,1:T(8,128)(2,1)S(1)}, bf16[1024,512]{0,1:T(8,128)(2,1)S(1)}, u32[]{:S(2)}, u32[]{:S(2)}) %collective-permute-start.53) | collective-permute-done | bytes 1048608 | tf_op jit(solution)/shard_map/ppermute | solution.py:31
  416.9 29.4 %collective-permute-done.52 = bf16[1024,512]{0,1:T(8,128)(2,1)S(1)} collective-permute-done((bf16[1024,512]{0,1:T(8,128)(2,1)S(1)}, bf16[1024,512]{0,1:T(8,128)(2,1)S(1)}, u32[]{:S(2)}, u32[]{:S(2)}) %collective-permute-start.52) | collective-permute-done | bytes 1048608 | tf_op jit(solution)/shard_map/ppermute | solution.py:31
  (142 shorter events, 49.7 us)
Async XLA Ops:
  0.0 5.8 %collective-permute-start = (bf16[128,512]{1,0:T(8,128)(2,1)}, bf16[128,512]{1,0:T(8,128)(2,1)S(1)}, u32[]{:S(2)}, u32[]{:S(2)}) collective-permute-start(bf16[128,512]{1,0:T(8,128)(2,1)} %bitcast.97), channel_id=1, source_target_pairs={{0,1},{1,2},{2,3},{3,4},{4,5},{5,6},{6,7},{7,0},{8,9},{9,10},{10,1... | collective-permute-start | bytes 393224 | tf_op jit(solution)/shard_map/ppermute | solution.py:16
  0.0 6.0 %collective-permute-start.1 = (bf16[128,512]{1,0:T(8,128)(2,1)}, bf16[128,512]{1,0:T(8,128)(2,1)S(1)}, u32[]{:S(2)}, u32[]{:S(2)}) collective-permute-start(bf16[128,512]{1,0:T(8,128)(2,1)} %bitcast.98), channel_id=1, source_target_pairs={{0,7},{1,0},{2,1},{3,2},{4,3},{5,4},{6,5},{7,6},{8,15},{9,8},{10,9... | collective-permute-start | bytes 393224 | tf_op jit(solution)/shard_map/ppermute | solution.py:21
  5.9 5.6 %collective-permute-start.2 = (bf16[128,512]{1,0:T(8,128)(2,1)S(1)}, bf16[128,512]{1,0:T(8,128)(2,1)S(1)}, u32[]{:S(2)}, u32[]{:S(2)}) collective-permute-start(bf16[128,512]{1,0:T(8,128)(2,1)S(1)} %collective-permute-done), channel_id=1, source_target_pairs={{0,1},{1,2},{2,3},{3,4},{4,5},{5,6},{6,7},{7,0},{8,9},{9,10},{10,1... | collective-permute-start | bytes 393224 | tf_op jit(solution)/shard_map/ppermute | solution.py:16
  11.7 5.6 %collective-permute-start.4 = (bf16[128,512]{1,0:T(8,128)(2,1)S(1)}, bf16[128,512]{1,0:T(8,128)(2,1)S(1)}, u32[]{:S(2)}, u32[]{:S(2)}) collective-permute-start(bf16[128,512]{1,0:T(8,128)(2,1)S(1)} %collective-permute-done.2), channel_id=1, source_target_pairs={{0,1},{1,2},{2,3},{3,4},{4,5},{5,6},{6,7},{7,0},{8,9},{9,10},{10,1... | collective-permute-start | bytes 393224 | tf_op jit(solution)/shard_map/ppermute | solution.py:16
  11.9 5.6 %collective-permute-start.5 = (bf16[128,512]{1,0:T(8,128)(2,1)S(1)}, bf16[128,512]{1,0:T(8,128)(2,1)S(1)}, u32[]{:S(2)}, u32[]{:S(2)}) collective-permute-start(bf16[128,512]{1,0:T(8,128)(2,1)S(1)} %collective-permute-done.3), channel_id=1, source_target_pairs={{0,7},{1,0},{2,1},{3,2},{4,3},{5,4},{6,5},{7,6},{8,15},{9,8},{10,9... | collective-permute-start | bytes 393224 | tf_op jit(solution)/shard_map/ppermute | solution.py:21
  17.4 5.6 %collective-permute-start.6 = (bf16[128,512]{1,0:T(8,128)(2,1)S(1)}, bf16[128,512]{1,0:T(8,128)(2,1)S(1)}, u32[]{:S(2)}, u32[]{:S(2)}) collective-permute-start(bf16[128,512]{1,0:T(8,128)(2,1)S(1)} %collective-permute-done.4), channel_id=1, source_target_pairs={{0,1},{1,2},{2,3},{3,4},{4,5},{5,6},{6,7},{7,0},{8,9},{9,10},{10,1... | collective-permute-start | bytes 393224 | tf_op jit(solution)/shard_map/ppermute | solution.py:16
  23.2 29.3 %collective-permute-start.8 = (bf16[1024,512]{0,1:T(8,128)(2,1)S(1)}, bf16[1024,512]{0,1:T(8,128)(2,1)S(1)}, u32[]{:S(2)}, u32[]{:S(2)}) collective-permute-start(bf16[1024,512]{0,1:T(8,128)(2,1)S(1)} %constant_dynamic-update-slice_fusion.40), channel_id=1, source_target_pairs={{8,0},{16,8},{24,16},{32,24},{40,32},{48,40},{56,48},{64,56},{72,6... | collective-permute-start | bytes 3145736 | tf_op jit(solution)/shard_map/ppermute | solution.py:31
  34.2 25.7 %collective-permute-start.7 = (bf16[1024,512]{0,1:T(8,128)(2,1)S(1)}, bf16[1024,512]{0,1:T(8,128)(2,1)S(1)}, u32[]{:S(2)}, u32[]{:S(2)}) collective-permute-start(bf16[1024,512]{0,1:T(8,128)(2,1)S(1)} %constant_dynamic-update-slice_fusion.40), channel_id=1, source_target_pairs={{0,8},{8,16},{16,24},{24,32},{32,40},{40,48},{48,56},{56,64},{64,7... | collective-permute-start | bytes 3145736 | tf_op jit(solution)/shard_map/ppermute | solution.py:31
  61.0 5.6 %collective-permute-start.9 = (bf16[128,512]{0,1:T(8,128)(2,1)S(1)}, bf16[128,512]{0,1:T(8,128)(2,1)S(1)}, u32[]{:S(2)}, u32[]{:S(2)}) collective-permute-start(bf16[128,512]{0,1:T(8,128)(2,1)S(1)} %get-tuple-element.6), channel_id=1, source_target_pairs={{0,1},{1,2},{2,3},{3,4},{4,5},{5,6},{6,7},{7,0},{8,9},{9,10},{10,1... | collective-permute-start | bytes 393224 | tf_op jit(solution)/shard_map/ppermute | solution.py:16
  61.1 5.6 %collective-permute-start.10 = (bf16[128,512]{0,1:T(8,128)(2,1)S(1)}, bf16[128,512]{0,1:T(8,128)(2,1)S(1)}, u32[]{:S(2)}, u32[]{:S(2)}) collective-permute-start(bf16[128,512]{0,1:T(8,128)(2,1)S(1)} %get-tuple-element.6), channel_id=1, source_target_pairs={{0,7},{1,0},{2,1},{3,2},{4,3},{5,4},{6,5},{7,6},{8,15},{9,8},{10,9... | collective-permute-start | bytes 393224 | tf_op jit(solution)/shard_map/ppermute | solution.py:21
  66.6 5.6 %collective-permute-start.11 = (bf16[128,512]{0,1:T(8,128)(2,1)S(1)}, bf16[128,512]{0,1:T(8,128)(2,1)S(1)}, u32[]{:S(2)}, u32[]{:S(2)}) collective-permute-start(bf16[128,512]{0,1:T(8,128)(2,1)S(1)} %collective-permute-done.9), channel_id=1, source_target_pairs={{0,1},{1,2},{2,3},{3,4},{4,5},{5,6},{6,7},{7,0},{8,9},{9,10},{10,1... | collective-permute-start | bytes 393224 | tf_op jit(solution)/shard_map/ppermute | solution.py:16
  72.2 5.6 %collective-permute-start.13 = (bf16[128,512]{0,1:T(8,128)(2,1)S(1)}, bf16[128,512]{0,1:T(8,128)(2,1)S(1)}, u32[]{:S(2)}, u32[]{:S(2)}) collective-permute-start(bf16[128,512]{0,1:T(8,128)(2,1)S(1)} %collective-permute-done.11), channel_id=1, source_target_pairs={{0,1},{1,2},{2,3},{3,4},{4,5},{5,6},{6,7},{7,0},{8,9},{9,10},{10,1... | collective-permute-start | bytes 393224 | tf_op jit(solution)/shard_map/ppermute | solution.py:16
  72.3 5.6 %collective-permute-start.14 = (bf16[128,512]{0,1:T(8,128)(2,1)S(1)}, bf16[128,512]{0,1:T(8,128)(2,1)S(1)}, u32[]{:S(2)}, u32[]{:S(2)}) collective-permute-start(bf16[128,512]{0,1:T(8,128)(2,1)S(1)} %collective-permute-done.12), channel_id=1, source_target_pairs={{0,7},{1,0},{2,1},{3,2},{4,3},{5,4},{6,5},{7,6},{8,15},{9,8},{10,9... | collective-permute-start | bytes 393224 | tf_op jit(solution)/shard_map/ppermute | solution.py:21
  77.8 5.6 %collective-permute-start.15 = (bf16[128,512]{0,1:T(8,128)(2,1)S(1)}, bf16[128,512]{0,1:T(8,128)(2,1)S(1)}, u32[]{:S(2)}, u32[]{:S(2)}) collective-permute-start(bf16[128,512]{0,1:T(8,128)(2,1)S(1)} %collective-permute-done.13), channel_id=1, source_target_pairs={{0,1},{1,2},{2,3},{3,4},{4,5},{5,6},{6,7},{7,0},{8,9},{9,10},{10,1... | collective-permute-start | bytes 393224 | tf_op jit(solution)/shard_map/ppermute | solution.py:16
  83.5 46.2 %collective-permute-start.17 = (bf16[1024,512]{0,1:T(8,128)(2,1)S(1)}, bf16[1024,512]{0,1:T(8,128)(2,1)S(1)}, u32[]{:S(2)}, u32[]{:S(2)}) collective-permute-start(bf16[1024,512]{0,1:T(8,128)(2,1)S(1)} %constant_dynamic-update-slice_fusion.32), channel_id=1, source_target_pairs={{16,0},{24,8},{32,16},{40,24},{48,32},{56,40},{64,48},{72,56},{80,... | collective-permute-start | bytes 3145736 | tf_op jit(solution)/shard_map/ppermute | solution.py:31
  85.4 48.8 %collective-permute-start.16 = (bf16[1024,512]{0,1:T(8,128)(2,1)S(1)}, bf16[1024,512]{0,1:T(8,128)(2,1)S(1)}, u32[]{:S(2)}, u32[]{:S(2)}) collective-permute-start(bf16[1024,512]{0,1:T(8,128)(2,1)S(1)} %constant_dynamic-update-slice_fusion.32), channel_id=1, source_target_pairs={{0,16},{8,24},{16,32},{24,40},{32,48},{40,56},{48,64},{56,72},{64,... | collective-permute-start | bytes 3145736 | tf_op jit(solution)/shard_map/ppermute | solution.py:31
  135.3 5.6 %collective-permute-start.18 = (bf16[128,512]{0,1:T(8,128)(2,1)S(1)}, bf16[128,512]{0,1:T(8,128)(2,1)S(1)}, u32[]{:S(2)}, u32[]{:S(2)}) collective-permute-start(bf16[128,512]{0,1:T(8,128)(2,1)S(1)} %get-tuple-element.8), channel_id=1, source_target_pairs={{0,1},{1,2},{2,3},{3,4},{4,5},{5,6},{6,7},{7,0},{8,9},{9,10},{10,1... | collective-permute-start | bytes 393224 | tf_op jit(solution)/shard_map/ppermute | solution.py:16
  135.4 5.6 %collective-permute-start.19 = (bf16[128,512]{0,1:T(8,128)(2,1)S(1)}, bf16[128,512]{0,1:T(8,128)(2,1)S(1)}, u32[]{:S(2)}, u32[]{:S(2)}) collective-permute-start(bf16[128,512]{0,1:T(8,128)(2,1)S(1)} %get-tuple-element.8), channel_id=1, source_target_pairs={{0,7},{1,0},{2,1},{3,2},{4,3},{5,4},{6,5},{7,6},{8,15},{9,8},{10,9... | collective-permute-start | bytes 393224 | tf_op jit(solution)/shard_map/ppermute | solution.py:21
  140.9 5.6 %collective-permute-start.20 = (bf16[128,512]{0,1:T(8,128)(2,1)S(1)}, bf16[128,512]{0,1:T(8,128)(2,1)S(1)}, u32[]{:S(2)}, u32[]{:S(2)}) collective-permute-start(bf16[128,512]{0,1:T(8,128)(2,1)S(1)} %collective-permute-done.18), channel_id=1, source_target_pairs={{0,1},{1,2},{2,3},{3,4},{4,5},{5,6},{6,7},{7,0},{8,9},{9,10},{10,1... | collective-permute-start | bytes 393224 | tf_op jit(solution)/shard_map/ppermute | solution.py:16
  141.0 5.6 %collective-permute-start.21 = (bf16[128,512]{0,1:T(8,128)(2,1)S(1)}, bf16[128,512]{0,1:T(8,128)(2,1)S(1)}, u32[]{:S(2)}, u32[]{:S(2)}) collective-permute-start(bf16[128,512]{0,1:T(8,128)(2,1)S(1)} %collective-permute-done.19), channel_id=1, source_target_pairs={{0,7},{1,0},{2,1},{3,2},{4,3},{5,4},{6,5},{7,6},{8,15},{9,8},{10,9... | collective-permute-start | bytes 393224 | tf_op jit(solution)/shard_map/ppermute | solution.py:21
  146.6 5.6 %collective-permute-start.22 = (bf16[128,512]{0,1:T(8,128)(2,1)S(1)}, bf16[128,512]{0,1:T(8,128)(2,1)S(1)}, u32[]{:S(2)}, u32[]{:S(2)}) collective-permute-start(bf16[128,512]{0,1:T(8,128)(2,1)S(1)} %collective-permute-done.20), channel_id=1, source_target_pairs={{0,1},{1,2},{2,3},{3,4},{4,5},{5,6},{6,7},{7,0},{8,9},{9,10},{10,1... | collective-permute-start | bytes 393224 | tf_op jit(solution)/shard_map/ppermute | solution.py:16
  146.6 5.6 %collective-permute-start.23 = (bf16[128,512]{0,1:T(8,128)(2,1)S(1)}, bf16[128,512]{0,1:T(8,128)(2,1)S(1)}, u32[]{:S(2)}, u32[]{:S(2)}) collective-permute-start(bf16[128,512]{0,1:T(8,128)(2,1)S(1)} %collective-permute-done.21), channel_id=1, source_target_pairs={{0,7},{1,0},{2,1},{3,2},{4,3},{5,4},{6,5},{7,6},{8,15},{9,8},{10,9... | collective-permute-start | bytes 393224 | tf_op jit(solution)/shard_map/ppermute | solution.py:21
  152.2 5.6 %collective-permute-start.24 = (bf16[128,512]{0,1:T(8,128)(2,1)S(1)}, bf16[128,512]{0,1:T(8,128)(2,1)S(1)}, u32[]{:S(2)}, u32[]{:S(2)}) collective-permute-start(bf16[128,512]{0,1:T(8,128)(2,1)S(1)} %collective-permute-done.22), channel_id=1, source_target_pairs={{0,1},{1,2},{2,3},{3,4},{4,5},{5,6},{6,7},{7,0},{8,9},{9,10},{10,1... | collective-permute-start | bytes 393224 | tf_op jit(solution)/shard_map/ppermute | solution.py:16
  157.8 92.1 %collective-permute-start.26 = (bf16[1024,512]{0,1:T(8,128)(2,1)S(1)}, bf16[1024,512]{0,1:T(8,128)(2,1)S(1)}, u32[]{:S(2)}, u32[]{:S(2)}) collective-permute-start(bf16[1024,512]{0,1:T(8,128)(2,1)S(1)} %constant_dynamic-update-slice_fusion.24), channel_id=1, source_target_pairs={{32,0},{40,8},{48,16},{56,24},{64,32},{72,40},{80,48},{88,56},{96,... | collective-permute-start | bytes 3145736 | tf_op jit(solution)/shard_map/ppermute | solution.py:31
  159.7 90.7 %collective-permute-start.25 = (bf16[1024,512]{0,1:T(8,128)(2,1)S(1)}, bf16[1024,512]{0,1:T(8,128)(2,1)S(1)}, u32[]{:S(2)}, u32[]{:S(2)}) collective-permute-start(bf16[1024,512]{0,1:T(8,128)(2,1)S(1)} %constant_dynamic-update-slice_fusion.24), channel_id=1, source_target_pairs={{0,32},{8,40},{16,48},{24,56},{32,64},{40,72},{48,80},{56,88},{64,... | collective-permute-start | bytes 3145736 | tf_op jit(solution)/shard_map/ppermute | solution.py:31
  251.5 5.6 %collective-permute-start.27 = (bf16[128,512]{0,1:T(8,128)(2,1)S(1)}, bf16[128,512]{0,1:T(8,128)(2,1)S(1)}, u32[]{:S(2)}, u32[]{:S(2)}) collective-permute-start(bf16[128,512]{0,1:T(8,128)(2,1)S(1)} %get-tuple-element.10), channel_id=1, source_target_pairs={{0,1},{1,2},{2,3},{3,4},{4,5},{5,6},{6,7},{7,0},{8,9},{9,10},{10,1... | collective-permute-start | bytes 393224 | tf_op jit(solution)/shard_map/ppermute | solution.py:16
  251.5 5.6 %collective-permute-start.28 = (bf16[128,512]{0,1:T(8,128)(2,1)S(1)}, bf16[128,512]{0,1:T(8,128)(2,1)S(1)}, u32[]{:S(2)}, u32[]{:S(2)}) collective-permute-start(bf16[128,512]{0,1:T(8,128)(2,1)S(1)} %get-tuple-element.10), channel_id=1, source_target_pairs={{0,7},{1,0},{2,1},{3,2},{4,3},{5,4},{6,5},{7,6},{8,15},{9,8},{10,9... | collective-permute-start | bytes 393224 | tf_op jit(solution)/shard_map/ppermute | solution.py:21
  257.1 5.6 %collective-permute-start.29 = (bf16[128,512]{0,1:T(8,128)(2,1)S(1)}, bf16[128,512]{0,1:T(8,128)(2,1)S(1)}, u32[]{:S(2)}, u32[]{:S(2)}) collective-permute-start(bf16[128,512]{0,1:T(8,128)(2,1)S(1)} %collective-permute-done.27), channel_id=1, source_target_pairs={{0,1},{1,2},{2,3},{3,4},{4,5},{5,6},{6,7},{7,0},{8,9},{9,10},{10,1... | collective-permute-start | bytes 393224 | tf_op jit(solution)/shard_map/ppermute | solution.py:16
  257.1 5.6 %collective-permute-start.30 = (bf16[128,512]{0,1:T(8,128)(2,1)S(1)}, bf16[128,512]{0,1:T(8,128)(2,1)S(1)}, u32[]{:S(2)}, u32[]{:S(2)}) collective-permute-start(bf16[128,512]{0,1:T(8,128)(2,1)S(1)} %collective-permute-done.28), channel_id=1, source_target_pairs={{0,7},{1,0},{2,1},{3,2},{4,3},{5,4},{6,5},{7,6},{8,15},{9,8},{10,9... | collective-permute-start | bytes 393224 | tf_op jit(solution)/shard_map/ppermute | solution.py:21
  262.7 5.6 %collective-permute-start.31 = (bf16[128,512]{0,1:T(8,128)(2,1)S(1)}, bf16[128,512]{0,1:T(8,128)(2,1)S(1)}, u32[]{:S(2)}, u32[]{:S(2)}) collective-permute-start(bf16[128,512]{0,1:T(8,128)(2,1)S(1)} %collective-permute-done.29), channel_id=1, source_target_pairs={{0,1},{1,2},{2,3},{3,4},{4,5},{5,6},{6,7},{7,0},{8,9},{9,10},{10,1... | collective-permute-start | bytes 393224 | tf_op jit(solution)/shard_map/ppermute | solution.py:16
  262.7 5.6 %collective-permute-start.32 = (bf16[128,512]{0,1:T(8,128)(2,1)S(1)}, bf16[128,512]{0,1:T(8,128)(2,1)S(1)}, u32[]{:S(2)}, u32[]{:S(2)}) collective-permute-start(bf16[128,512]{0,1:T(8,128)(2,1)S(1)} %collective-permute-done.30), channel_id=1, source_target_pairs={{0,7},{1,0},{2,1},{3,2},{4,3},{5,4},{6,5},{7,6},{8,15},{9,8},{10,9... | collective-permute-start | bytes 393224 | tf_op jit(solution)/shard_map/ppermute | solution.py:21
  268.3 5.6 %collective-permute-start.33 = (bf16[128,512]{0,1:T(8,128)(2,1)S(1)}, bf16[128,512]{0,1:T(8,128)(2,1)S(1)}, u32[]{:S(2)}, u32[]{:S(2)}) collective-permute-start(bf16[128,512]{0,1:T(8,128)(2,1)S(1)} %collective-permute-done.31), channel_id=1, source_target_pairs={{0,1},{1,2},{2,3},{3,4},{4,5},{5,6},{6,7},{7,0},{8,9},{9,10},{10,1... | collective-permute-start | bytes 393224 | tf_op jit(solution)/shard_map/ppermute | solution.py:16
  273.9 22.7 %collective-permute-start.35 = (bf16[1024,512]{0,1:T(8,128)(2,1)S(1)}, bf16[1024,512]{0,1:T(8,128)(2,1)S(1)}, u32[]{:S(2)}, u32[]{:S(2)}) collective-permute-start(bf16[1024,512]{0,1:T(8,128)(2,1)S(1)} %constant_dynamic-update-slice_fusion.16), channel_id=1, source_target_pairs={{64,0},{72,8},{80,16},{88,24},{96,32},{104,40},{112,48},{120,56},{... | collective-permute-start | bytes 3145736 | tf_op jit(solution)/shard_map/ppermute | solution.py:31
  275.9 23.9 %collective-permute-start.34 = (bf16[1024,512]{0,1:T(8,128)(2,1)S(1)}, bf16[1024,512]{0,1:T(8,128)(2,1)S(1)}, u32[]{:S(2)}, u32[]{:S(2)}) collective-permute-start(bf16[1024,512]{0,1:T(8,128)(2,1)S(1)} %constant_dynamic-update-slice_fusion.16), channel_id=1, source_target_pairs={{0,64},{8,72},{16,80},{24,88},{32,96},{40,104},{48,112},{56,120},{... | collective-permute-start | bytes 3145736 | tf_op jit(solution)/shard_map/ppermute | solution.py:31
  300.9 5.6 %collective-permute-start.36 = (bf16[128,512]{0,1:T(8,128)(2,1)S(1)}, bf16[128,512]{0,1:T(8,128)(2,1)S(1)}, u32[]{:S(2)}, u32[]{:S(2)}) collective-permute-start(bf16[128,512]{0,1:T(8,128)(2,1)S(1)} %get-tuple-element.12), channel_id=1, source_target_pairs={{0,1},{1,2},{2,3},{3,4},{4,5},{5,6},{6,7},{7,0},{8,9},{9,10},{10,1... | collective-permute-start | bytes 393224 | tf_op jit(solution)/shard_map/ppermute | solution.py:16
  300.9 5.6 %collective-permute-start.37 = (bf16[128,512]{0,1:T(8,128)(2,1)S(1)}, bf16[128,512]{0,1:T(8,128)(2,1)S(1)}, u32[]{:S(2)}, u32[]{:S(2)}) collective-permute-start(bf16[128,512]{0,1:T(8,128)(2,1)S(1)} %get-tuple-element.12), channel_id=1, source_target_pairs={{0,7},{1,0},{2,1},{3,2},{4,3},{5,4},{6,5},{7,6},{8,15},{9,8},{10,9... | collective-permute-start | bytes 393224 | tf_op jit(solution)/shard_map/ppermute | solution.py:21
  306.5 5.6 %collective-permute-start.38 = (bf16[128,512]{0,1:T(8,128)(2,1)S(1)}, bf16[128,512]{0,1:T(8,128)(2,1)S(1)}, u32[]{:S(2)}, u32[]{:S(2)}) collective-permute-start(bf16[128,512]{0,1:T(8,128)(2,1)S(1)} %collective-permute-done.36), channel_id=1, source_target_pairs={{0,1},{1,2},{2,3},{3,4},{4,5},{5,6},{6,7},{7,0},{8,9},{9,10},{10,1... | collective-permute-start | bytes 393224 | tf_op jit(solution)/shard_map/ppermute | solution.py:16
  312.1 5.6 %collective-permute-start.40 = (bf16[128,512]{0,1:T(8,128)(2,1)S(1)}, bf16[128,512]{0,1:T(8,128)(2,1)S(1)}, u32[]{:S(2)}, u32[]{:S(2)}) collective-permute-start(bf16[128,512]{0,1:T(8,128)(2,1)S(1)} %collective-permute-done.38), channel_id=1, source_target_pairs={{0,1},{1,2},{2,3},{3,4},{4,5},{5,6},{6,7},{7,0},{8,9},{9,10},{10,1... | collective-permute-start | bytes 393224 | tf_op jit(solution)/shard_map/ppermute | solution.py:16
  317.7 5.6 %collective-permute-start.42 = (bf16[128,512]{0,1:T(8,128)(2,1)S(1)}, bf16[128,512]{0,1:T(8,128)(2,1)S(1)}, u32[]{:S(2)}, u32[]{:S(2)}) collective-permute-start(bf16[128,512]{0,1:T(8,128)(2,1)S(1)} %collective-permute-done.40), channel_id=1, source_target_pairs={{0,1},{1,2},{2,3},{3,4},{4,5},{5,6},{6,7},{7,0},{8,9},{9,10},{10,1... | collective-permute-start | bytes 393224 | tf_op jit(solution)/shard_map/ppermute | solution.py:16
  323.3 46.0 %collective-permute-start.44 = (bf16[1024,512]{0,1:T(8,128)(2,1)S(1)}, bf16[1024,512]{0,1:T(8,128)(2,1)S(1)}, u32[]{:S(2)}, u32[]{:S(2)}) collective-permute-start(bf16[1024,512]{0,1:T(8,128)(2,1)S(1)} %constant_dynamic-update-slice_fusion.8), channel_id=1, source_target_pairs={{128,0},{136,8},{144,16},{152,24},{160,32},{168,40},{176,48},{184,... | collective-permute-start | bytes 3145736 | tf_op jit(solution)/shard_map/ppermute | solution.py:31
  325.3 47.2 %collective-permute-start.43 = (bf16[1024,512]{0,1:T(8,128)(2,1)S(1)}, bf16[1024,512]{0,1:T(8,128)(2,1)S(1)}, u32[]{:S(2)}, u32[]{:S(2)}) collective-permute-start(bf16[1024,512]{0,1:T(8,128)(2,1)S(1)} %constant_dynamic-update-slice_fusion.8), channel_id=1, source_target_pairs={{0,128},{8,136},{16,144},{24,152},{32,160},{40,168},{48,176},{56,1... | collective-permute-start | bytes 3145736 | tf_op jit(solution)/shard_map/ppermute | solution.py:31
  373.6 5.6 %collective-permute-start.45 = (bf16[128,512]{0,1:T(8,128)(2,1)S(1)}, bf16[128,512]{0,1:T(8,128)(2,1)S(1)}, u32[]{:S(2)}, u32[]{:S(2)}) collective-permute-start(bf16[128,512]{0,1:T(8,128)(2,1)S(1)} %get-tuple-element.14), channel_id=1, source_target_pairs={{0,1},{1,2},{2,3},{3,4},{4,5},{5,6},{6,7},{7,0},{8,9},{9,10},{10,1... | collective-permute-start | bytes 393224 | tf_op jit(solution)/shard_map/ppermute | solution.py:16
  373.6 5.6 %collective-permute-start.46 = (bf16[128,512]{0,1:T(8,128)(2,1)S(1)}, bf16[128,512]{0,1:T(8,128)(2,1)S(1)}, u32[]{:S(2)}, u32[]{:S(2)}) collective-permute-start(bf16[128,512]{0,1:T(8,128)(2,1)S(1)} %get-tuple-element.14), channel_id=1, source_target_pairs={{0,7},{1,0},{2,1},{3,2},{4,3},{5,4},{6,5},{7,6},{8,15},{9,8},{10,9... | collective-permute-start | bytes 393224 | tf_op jit(solution)/shard_map/ppermute | solution.py:21
  379.2 5.6 %collective-permute-start.47 = (bf16[128,512]{0,1:T(8,128)(2,1)S(1)}, bf16[128,512]{0,1:T(8,128)(2,1)S(1)}, u32[]{:S(2)}, u32[]{:S(2)}) collective-permute-start(bf16[128,512]{0,1:T(8,128)(2,1)S(1)} %collective-permute-done.45), channel_id=1, source_target_pairs={{0,1},{1,2},{2,3},{3,4},{4,5},{5,6},{6,7},{7,0},{8,9},{9,10},{10,1... | collective-permute-start | bytes 393224 | tf_op jit(solution)/shard_map/ppermute | solution.py:16
  384.8 5.6 %collective-permute-start.49 = (bf16[128,512]{0,1:T(8,128)(2,1)S(1)}, bf16[128,512]{0,1:T(8,128)(2,1)S(1)}, u32[]{:S(2)}, u32[]{:S(2)}) collective-permute-start(bf16[128,512]{0,1:T(8,128)(2,1)S(1)} %collective-permute-done.47), channel_id=1, source_target_pairs={{0,1},{1,2},{2,3},{3,4},{4,5},{5,6},{6,7},{7,0},{8,9},{9,10},{10,1... | collective-permute-start | bytes 393224 | tf_op jit(solution)/shard_map/ppermute | solution.py:16
  390.4 5.6 %collective-permute-start.51 = (bf16[128,512]{0,1:T(8,128)(2,1)S(1)}, bf16[128,512]{0,1:T(8,128)(2,1)S(1)}, u32[]{:S(2)}, u32[]{:S(2)}) collective-permute-start(bf16[128,512]{0,1:T(8,128)(2,1)S(1)} %collective-permute-done.49), channel_id=1, source_target_pairs={{0,1},{1,2},{2,3},{3,4},{4,5},{5,6},{6,7},{7,0},{8,9},{9,10},{10,1... | collective-permute-start | bytes 393224 | tf_op jit(solution)/shard_map/ppermute | solution.py:16
  396.0 20.4 %collective-permute-start.53 = (bf16[1024,512]{0,1:T(8,128)(2,1)S(1)}, bf16[1024,512]{0,1:T(8,128)(2,1)S(1)}, u32[]{:S(2)}, u32[]{:S(2)}) collective-permute-start(bf16[1024,512]{0,1:T(8,128)(2,1)S(1)} %constant_dynamic-update-slice_fusion), channel_id=1, source_target_pairs={{256,0},{264,8},{272,16},{280,24},{288,32},{296,40},{304,48},{312,... | collective-permute-start | bytes 3145736 | tf_op jit(solution)/shard_map/ppermute | solution.py:31
  397.4 49.0 %collective-permute-start.52 = (bf16[1024,512]{0,1:T(8,128)(2,1)S(1)}, bf16[1024,512]{0,1:T(8,128)(2,1)S(1)}, u32[]{:S(2)}, u32[]{:S(2)}) collective-permute-start(bf16[1024,512]{0,1:T(8,128)(2,1)S(1)} %constant_dynamic-update-slice_fusion), channel_id=1, source_target_pairs={{0,256},{8,264},{16,272},{24,280},{32,288},{40,296},{48,304},{56,3... | collective-permute-start | bytes 3145736 | tf_op jit(solution)/shard_map/ppermute | solution.py:31
  (9 other events, 124.4 us)
